TPU v7x, 128 devices: a whole 4x4x4 slice. The times are simulated.
128 devices in a mesh: grp: 2 (over core), fsdp: 64 (over x, y, z).
Axes of the slice: x: 4, y: 4, z: 4, core: 2. Of those that a mesh axis runs over, the one named last changes fastest.
Arguments:
- item_states: bfloat16 [512, 256, 2048], P(('grp', 'fsdp')), may hold values from -6 to 6
- w_query: bfloat16 [2048, 2048], P('fsdp'), may hold values from -0.125 to 0.125
- w_key: bfloat16 [2048, 256], P('fsdp'), may hold values from -0.125 to 0.125
- w_value: bfloat16 [2048, 256], P('fsdp'), may hold values from -0.125 to 0.125
- item_gain: float32 [2048], replicated, may hold values from 0.25 to 1.75
- w_adapt: bfloat16 [2048, 4096], P('fsdp'), may hold values from -0.125 to 0.125
- user_gain: float32 [4096], replicated, may hold values from 0.25 to 1.75
- user_query: bfloat16 [4096, 128], P('fsdp'), may hold values from -0.5 to 0.5
- hist_owner: int32 [128, 128, 1], P(('grp', 'fsdp')), may hold values from 0 to 127; in each aligned block of 128 rows (0 to 127, 128 to 255, ..., all dimensions but the last counted through in order) at most 2 rows name the same one
- history_position_index: int32 [128, 128], P(('grp', 'fsdp')), may hold values from 0 to 3
- cotangent: bfloat16 [128, 128, 4096], P(('grp', 'fsdp')), may hold values from -6 to 6
Outputs:
- item_embed: bfloat16 [512, 2048], P(('grp', 'fsdp'))
- user_attention_output: bfloat16 [128, 128, 4096], P(('grp', 'fsdp'))
- item_grad: float32 [512, 2048], P(('grp', 'fsdp'))
Inputs may be any that keep to these rules, and one draw needn't show every extreme that they name: `hist_owner`: within one history no device is named by more than 2 positions, and some device is named by exactly 2 positions.
All inputs are finite; a program needn't handle non-finite values.
Results may differ from a plain program's by a relative error of at most 0.011.
Values may be sent and summed in bfloat16 or wider, within the bound.
No kernel may reach another device: no remote copies, remote signals or barrier semaphores. Data moves between devices by JAX's collectives and lax.ppermute only.
A program may use at most 128 MiB of HBM per device.

v0:
```python
import jax
import jax.numpy as jnp
from jax import lax
from jax.sharding import PartitionSpec as P

DI = 2048
IHEADS = 32
IHD = 64
IKV = 4
UHEADS = 32
UHD = 128
ILEN = 256


def stored(values):
    return lax.optimization_barrier(values.astype(jnp.bfloat16))


def rms_scale(values, gain):
    mean_sq = jnp.mean(values * values, axis=-1, keepdims=True)
    return values * lax.rsqrt(mean_sq + 1e-05) * gain


def item_pool(states, key_rows, value_rows, query_rows, item_gain):
    count = states.shape[0]
    group = IHEADS // IKV
    query_heads = query_rows.reshape(count, IKV, group, IHD).astype(jnp.float32)
    key_heads = key_rows.reshape(count, ILEN, IKV, IHD).astype(jnp.float32)
    value_heads = value_rows.reshape(count, ILEN, IKV, IHD).astype(jnp.float32)
    scores = jnp.einsum("igrd,itgd->igrt", query_heads, key_heads) * IHD ** (-0.5)
    weights = stored(jax.nn.softmax(scores, axis=-1)).astype(jnp.float32)
    mixed = jnp.einsum("igrt,itgd->igrd", weights, value_heads).reshape(count, IHEADS * IHD)
    last_row = states[:, ILEN - 1, :].astype(jnp.float32)
    return rms_scale(last_row + mixed, item_gain).astype(jnp.bfloat16)


def user_layer(hidden, user_gain, user_query):
    length_total = hidden.shape[0]
    normed = stored(rms_scale(hidden.astype(jnp.float32), user_gain)).astype(jnp.float32)
    heads = normed.reshape(length_total, UHEADS, UHD)
    query_map = user_query.reshape(UHEADS, UHD, UHD).astype(jnp.float32)
    queries = stored(jnp.einsum("thd,hde->the", heads, query_map)).astype(jnp.float32)
    scores = jnp.einsum("the,she->hts", queries, heads) * UHD ** (-0.5)
    target = jnp.arange(length_total, dtype=jnp.int32)
    causal = target[None, :, None] >= target[None, None, :]
    scores = jnp.where(causal, scores, -1e30)
    weights = stored(jax.nn.softmax(scores, axis=-1)).astype(jnp.float32)
    mixed = jnp.einsum("hts,shd->thd", weights, heads).reshape(length_total, UHEADS * UHD)
    return (hidden.astype(jnp.float32) + mixed).astype(jnp.bfloat16)


def serve_rows(requests, lookup_matrix):
    chosen_items = (
        requests[..., None] == jnp.arange(lookup_matrix.shape[0], dtype=jnp.int32)
    ).astype(lookup_matrix.dtype)
    return jnp.einsum(
        "ltj,jy->lty", chosen_items, lookup_matrix, preferred_element_type=jnp.float32
    ).astype(lookup_matrix.dtype)


def per_device(
    item_states,
    w_query,
    w_key,
    w_value,
    item_gain,
    w_adapt,
    user_gain,
    user_query,
    hist_owner,
    history_position_index,
    cotangent,
):
    groups = lax.axis_size("grp")
    shards = lax.axis_size("fsdp")
    devices = groups * shards
    count = item_states.shape[0]
    flat = item_states.reshape(count * ILEN, DI)
    last_row = item_states[:, ILEN - 1, :]
    columns = flat
    key_sum = jnp.dot(
        columns,
        lax.all_gather(w_key, "fsdp", axis=0, tiled=True),
        preferred_element_type=jnp.float32,
    )
    summed_value = jnp.dot(
        columns,
        lax.all_gather(w_value, "fsdp", axis=0, tiled=True),
        preferred_element_type=jnp.float32,
    )
    columns = last_row
    query_sum = jnp.dot(
        columns,
        lax.all_gather(w_query, "fsdp", axis=0, tiled=True),
        preferred_element_type=jnp.float32,
    )
    adapter, query_map = (
        lax.all_gather(w_adapt, "fsdp", axis=0, tiled=True),
        lax.all_gather(user_query, "fsdp", axis=0, tiled=True),
    )
    item_embed = item_pool(
        item_states, stored(key_sum), stored(summed_value), stored(query_sum), item_gain
    )
    length_total = history_position_index.shape[1]
    cap_slots = max(2, 2 * length_total // devices)
    owner_users = hist_owner[0, :, 0]
    owner_hot = (owner_users[:, None] == jnp.arange(devices, dtype=jnp.int32)[None, :]).astype(
        jnp.int32
    )
    earlier = jnp.cumsum(owner_hot, axis=0) - owner_hot
    rank_in = jnp.sum(owner_hot * earlier, axis=1)
    position = owner_users * cap_slots + rank_in
    request = (
        jnp.full((devices * cap_slots,), count, jnp.int32)
        .at[position]
        .set(history_position_index[0])
    )
    request = request.reshape(devices, cap_slots)
    width = item_embed.shape[1]
    incoming = lax.all_to_all(request, ("grp", "fsdp"), split_axis=0, concat_axis=0, tiled=True)
    found = serve_rows(incoming, item_embed)
    returned = lax.all_to_all(found, ("grp", "fsdp"), split_axis=0, concat_axis=0, tiled=True)
    fetched = jnp.take(returned.reshape(devices * cap_slots, width), position, axis=0)
    hidden = stored(jnp.dot(fetched, adapter, preferred_element_type=jnp.float32))
    user_attention_output, pull = jax.vjp(
        lambda values: user_layer(values, user_gain, query_map), hidden
    )
    (grad_hidden,) = pull(cotangent[0])
    grad_rows = jnp.dot(grad_hidden, adapter.T, preferred_element_type=jnp.float32)
    outgoing = jnp.zeros((devices * cap_slots, DI), jnp.float32).at[position].set(grad_rows)
    arrived = lax.all_to_all(
        outgoing.reshape(devices, cap_slots, DI).astype(jnp.bfloat16),
        ("grp", "fsdp"),
        split_axis=0,
        concat_axis=0,
        tiled=True,
    ).astype(jnp.float32)
    terms = arrived.reshape(devices * cap_slots, DI)
    slot_hot = (
        incoming.reshape(-1)[:, None] == jnp.arange(count, dtype=jnp.int32)[None, :]
    ).astype(jnp.float32)
    item_grad = jnp.dot(slot_hot.T, terms, precision=lax.Precision.HIGHEST)
    return (item_embed, user_attention_output[None], item_grad)


def solution(mesh):
    placed = (
        P(("grp", "fsdp"), None, None),
        P("fsdp", None),
        P("fsdp", None),
        P("fsdp", None),
        P(),
        P("fsdp", None),
        P(),
        P("fsdp", None),
        P(("grp", "fsdp"), None, None),
        P(("grp", "fsdp"), None),
        P(("grp", "fsdp"), None, None),
    )
    return jax.shard_map(
        per_device,
        mesh=mesh,
        in_specs=placed,
        out_specs=(
            P(("grp", "fsdp"), None),
            P(("grp", "fsdp"), None, None),
            P(("grp", "fsdp"), None),
        ),
        check_vma=False,
    )
```

profile of v0, /device:TPU:1, one launch (start us, length us, event | category | flops | bytes accessed | tf_op | source)
XLA Modules:
  0.0 473.3 jit_solution(699172735839082642)
XLA Ops:
  7.2 0.7 all-gather.8.cloned.1.call-update
  7.9 0.7 all-gather.10.cloned.1.call-update
  8.7 0.7 all-gather.6.cloned.1.call-update
  9.4 0.5 all-gather.12.cloned.1.call-update
  10.0 0.7 fusion.54
  10.7 0.2 reduce_window_sum.11
  10.9 0.8 select_reduce_fusion
  11.7 0.7 fusion.58
  12.4 1.1 scatter_custom_fusion
  13.5 0.8 all_to_all.12
  14.3 11.5 %all-to-all-start = ((s32[128,1,2]{2,1,0:T(1,128)}), s32[128,1,2]{2,1,0:T(1,128)S(1)}, u32[]{:S(2)}, u32[]{:S(2)}) async-start(s32[128,1,2]{2,1,0:T(1,128)} %bitcast.7), calls=%async_computation | async-start | bytes 131072 | tf_op jit(solution)/shard_map/all_to_all | solution.py:120
  25.8 0.9 slice.4
  26.7 0.1 reshape.157
  26.8 8.2 %all-to-all-done = s32[128,1,2]{2,1,0:T(1,128)S(1)} async-done(((s32[128,1,2]{2,1,0:T(1,128)}), s32[128,1,2]{2,1,0:T(1,128)S(1)}, u32[]{:S(2)}, u32[]{:S(2)}) %all-to-all-start) | async-done | bytes 1056 | tf_op jit(solution)/shard_map/all_to_all | solution.py:120
  35.1 41.2 %all-gather.8.cloned.1.call-done = bf16[2048,256]{1,0:T(8,128)(2,1)} async-done(((bf16[32,256]{1,0:T(8,128)(2,1)}), bf16[2048,256]{1,0:T(8,128)(2,1)}) %all-gather.8.cloned.1.call-update) | async-done | bytes 1048592 | tf_op jit(solution)/shard_map/all_gather | solution.py:83
  76.3 3.7 convolution_convert_fusion.7
  80.0 0.4 reshape.183
  80.4 60.2 %all-gather.10.cloned.1.call-done = bf16[2048,256]{1,0:T(8,128)(2,1)} async-done(((bf16[32,256]{1,0:T(8,128)(2,1)}), bf16[2048,256]{1,0:T(8,128)(2,1)}) %all-gather.10.cloned.1.call-update) | async-done | bytes 1048592 | tf_op jit(solution)/shard_map/all_gather | solution.py:88
  140.7 3.7 convolution_convert_fusion.6
  144.4 0.4 reshape.184
  144.8 76.3 %all-gather.6.cloned.1.call-done = bf16[2048,2048]{1,0:T(8,128)(2,1)} async-done(((bf16[32,2048]{1,0:T(8,128)(2,1)}), bf16[2048,2048]{1,0:T(8,128)(2,1)}) %all-gather.6.cloned.1.call-update) | async-done | bytes 8388624 | tf_op jit(solution)/shard_map/all_gather | solution.py:94
  221.1 4.6 convolution_convert_fusion.2
  225.7 0.1 reshape.146
  225.8 0.6 fusion.75
  226.4 0.3 multiply_reduce_fusion
  227.0 0.5 convolution_convert_fusion.1
  227.5 2.0 copy.53
  229.5 8.0 %all-to-all-start.1 = ((bf16[128,2,2048]{2,1,0:T(2,128)(2,1)}), bf16[128,2,2048]{2,1,0:T(2,128)(2,1)S(1)}, u32[]{:S(2)}, u32[]{:S(2)}) async-start(bf16[128,2,2048]{2,1,0:T(2,128)(2,1)} %copy.53), calls=%async_computation.1 | async-start | bytes 2097152 | tf_op jit(solution)/shard_map/all_to_all | solution.py:122
  237.6 0.2 all-gather.14.cloned.1.call-start
  237.8 0.4 all-gather.14.cloned.1.call-update
  238.2 0.7 copy.79
  238.9 17.7 %all-to-all-done.1 = bf16[128,2,2048]{2,1,0:T(2,128)(2,1)S(1)} async-done(((bf16[128,2,2048]{2,1,0:T(2,128)(2,1)}), bf16[128,2,2048]{2,1,0:T(2,128)(2,1)S(1)}, u32[]{:S(2)}, u32[]{:S(2)}) %all-to-all-start.1) | async-done | bytes 1048608 | tf_op jit(solution)/shard_map/all_to_all | solution.py:122
  256.6 0.4 reshape.151
  257.1 0.9 gather_fusion
  258.0 78.2 %all-gather.12.cloned.1.call-done = bf16[2048,4096]{1,0:T(8,128)(2,1)} async-done(((bf16[32,4096]{1,0:T(8,128)(2,1)}), bf16[2048,4096]{1,0:T(8,128)(2,1)}) %all-gather.12.cloned.1.call-update) | async-done | bytes 16777232 | tf_op jit(solution)/shard_map/all_gather | solution.py:98
  336.2 8.2 %convolution_convert_fusion = bf16[128,4096]{1,0:T(8,128)(2,1)S(1)} fusion(bf16[2048,4096]{1,0:T(8,128)(2,1)} %all-gather.12.cloned.1.call-done, bf16[128,2048]{1,0:T(8,128)(2,1)S(1)} %gather_fusion, pred[128]{0:T(512)(128)(4,1)S(1)} %compare_and_fusion), kind=kOutput, calls=%fused_computation.5 | convolution fusion | flops 2148270080 | bytes 18350208 | tf_op jit(solution)/shard_map/dot_general | solution.py:124
  344.4 0.3 fusion.9
  344.7 0.3 fusion.11
  345.0 55.9 %all-gather.14.cloned.1.call-done = bf16[4096,128]{1,0:T(8,128)(2,1)} async-done(((bf16[64,128]{1,0:T(8,128)(2,1)}), bf16[4096,128]{1,0:T(8,128)(2,1)}) %all-gather.14.cloned.1.call-update) | async-done | bytes 1048592 | tf_op jit(solution)/shard_map/all_gather | solution.py:99
  400.9 2.6 fusion.15
  403.5 1.4 fusion.16
  404.9 3.5 fusion.76
  408.5 2.6 fusion.7
  411.1 0.2 copy-done.4
  411.3 0.3 copy-done.5
  411.6 0.8 fusion.73
  412.4 0.8 fusion.17
  413.2 0.9 fusion.81
  414.1 1.9 fusion.29
  416.0 0.9 add_convert_fusion
  416.9 0.5 copy.80
  417.4 2.9 copy.78
  420.3 3.1 fusion.13
  423.4 12.5 %fusion.22 = f32[128,2048]{1,0:T(8,128)} fusion(bf16[2048,4096]{1,0:T(8,128)(2,1)} %all-gather.12.cloned.1.call-done, bf16[128,4096]{1,0:T(8,128)(2,1)S(1)} %convolution_convert_fusion, bf16[128,4096]{1,0:T(8,128)(2,1)S(1)} %copy.80, bf16[1,128,4096]{2,1,0:T(8,128)(2,1)S(1)} %copy-done.2, f32[128]{0:T(128)S(1)} %multiply_multiply_fusion, ...), kind=kOutput, calls=%fused_computation.47 | convolution fusion | flops 2152202240 | bytes 20988928 | tf_op jit(solution)/shard_map/dot_general | solution.py:129
  435.9 2.4 scatter_custom_fusion.1
  438.3 0.1 convert_element_type.129
  438.5 1.5 convert_element_type.130
  440.0 7.6 %all-to-all-start.2 = ((bf16[128,2,2048]{2,1,0:T(2,128)(2,1)}), bf16[128,2,2048]{2,1,0:T(2,128)(2,1)S(1)}, u32[]{:S(2)}, u32[]{:S(2)}) async-start(bf16[128,2,2048]{2,1,0:T(2,128)(2,1)} %convert_element_type.130), calls=%async_computation.2 | async-start | bytes 2097152 | tf_op jit(solution)/shard_map/all_to_all | solution.py:131
  447.6 0.5 broadcast.136
  448.1 0.8 reduce.4
  448.9 0.1 eq.50
  449.0 16.4 %all-to-all-done.2 = bf16[128,2,2048]{2,1,0:T(2,128)(2,1)S(1)} async-done(((bf16[128,2,2048]{2,1,0:T(2,128)(2,1)}), bf16[128,2,2048]{2,1,0:T(2,128)(2,1)S(1)}, u32[]{:S(2)}, u32[]{:S(2)}) %all-to-all-start.2) | async-done | bytes 1048608 | tf_op jit(solution)/shard_map/all_to_all | solution.py:131
  465.4 0.4 reshape.156
  465.8 1.0 fusion.52
  (35 shorter events, 0.6 us)
Async XLA Ops:
  7.2 69.1 %all-gather.8.cloned.1.call-start = ((), (), s32[]{:S(2)}) async-start(), calls=%async_computation.4 | async-start | bytes 1064960 | tf_op jit(solution)/shard_map/all_gather | solution.py:83
  7.9 132.8 %all-gather.10.cloned.1.call-start = ((), (), s32[]{:S(2)}) async-start(), calls=%async_computation.5 | async-start | bytes 1064960 | tf_op jit(solution)/shard_map/all_gather | solution.py:88
  8.6 212.4 %all-gather.6.cloned.1.call-start = ((), (), s32[]{:S(2)}) async-start(), calls=%async_computation.3 | async-start | bytes 8519680 | tf_op jit(solution)/shard_map/all_gather | solution.py:94
  9.4 326.8 %all-gather.12.cloned.1.call-start = ((), (), s32[]{:S(2)}) async-start(), calls=%async_computation.6 | async-start | bytes 17039360 | tf_op jit(solution)/shard_map/all_gather | solution.py:98
  14.3 20.8 %all-to-all-start = ((s32[128,1,2]{2,1,0:T(1,128)}), s32[128,1,2]{2,1,0:T(1,128)S(1)}, u32[]{:S(2)}, u32[]{:S(2)}) async-start(s32[128,1,2]{2,1,0:T(1,128)} %bitcast.7), calls=%async_computation | async-start | bytes 131072 | tf_op jit(solution)/shard_map/all_to_all | solution.py:120
  225.7 1.2 copy-start.8
  227.0 2.6 copy-start.7
  227.5 10.7 %copy-start.1 = (bf16[1,128,4096]{2,1,0:T(8,128)(2,1)S(1)}, bf16[1,128,4096]{2,1,0:T(8,128)(2,1)}, u32[]{:S(2)}) copy-start(bf16[1,128,4096]{2,1,0:T(8,128)(2,1)} %param.21) | copy-start | bytes 3145732
  229.5 9.3 %copy-start.9 = (s32[1,128,1]{1,2,0:T(1,128)S(1)}, s32[1,128,1]{1,2,0:T(1,128)}, u32[]{:S(2)}) copy-start(s32[1,128,1]{1,2,0:T(1,128)} %param.19) | copy-start | bytes 1540
  229.5 27.1 %all-to-all-start.1 = ((bf16[128,2,2048]{2,1,0:T(2,128)(2,1)}), bf16[128,2,2048]{2,1,0:T(2,128)(2,1)S(1)}, u32[]{:S(2)}, u32[]{:S(2)}) async-start(bf16[128,2,2048]{2,1,0:T(2,128)(2,1)} %copy.53), calls=%async_computation.1 | async-start | bytes 2097152 | tf_op jit(solution)/shard_map/all_to_all | solution.py:122
  237.6 163.3 %all-gather.14.cloned.1.call-start = ((), (), s32[]{:S(2)}) async-start(), calls=%async_computation.7 | async-start | bytes 1064960 | tf_op jit(solution)/shard_map/all_gather | solution.py:99
  258.0 86.7 %copy-start.6 = (f32[4096]{0:T(1024)S(1)}, f32[4096]{0:T(1024)}, u32[]{:S(2)}) copy-start(f32[4096]{0:T(1024)} %param.17) | copy-start | bytes 49156
  408.5 2.6 copy-start.3
  408.5 2.9 copy-start.4
  408.5 3.1 copy-start.5
  414.1 1.9 copy-start
  420.3 3.1 copy-start.2
  440.0 25.4 %all-to-all-start.2 = ((bf16[128,2,2048]{2,1,0:T(2,128)(2,1)}), bf16[128,2,2048]{2,1,0:T(2,128)(2,1)S(1)}, u32[]{:S(2)}, u32[]{:S(2)}) async-start(bf16[128,2,2048]{2,1,0:T(2,128)(2,1)} %convert_element_type.130), calls=%async_computation.2 | async-start | bytes 2097152 | tf_op jit(solution)/shard_map/all_to_all | solution.py:131
Sparse Core Ops, SparseCore 0:
  10.9 65.3 all-gather.7
  79.2 61.4 all-gather.9
  143.6 77.4 all-gather.5
  223.8 112.3 all-gather.11
  339.0 61.9 all-gather.13
where the time goes:
time: 474 us; the launch traced here: 473 us
  waiting for transfers between devices  357 us (75%)
  matrix products  47.8 us (10%)
  starting transfers between devices  27.4 us (6%)
  local copies, waits for them, and re-layouts  17 us (4%)
  between operations  14.1 us (3%)
  other arithmetic  9.93 us (2%)
    all_gather x1, waiting for transfers between devices, per_device(): lax.all_gather(w_adapt, 'fsdp', axis=0, tiled=True)  78.2 us
    all_gather x1, waiting for transfers between devices, per_device(): lax.all_gather(w_query, 'fsdp', axis=0, tiled=True)  76.3 us
    all_gather x1, waiting for transfers between devices, per_device(): lax.all_gather(w_value, 'fsdp', axis=0, tiled=True)  60.2 us
    all_gather x1, waiting for transfers between devices, per_device(): lax.all_gather(user_query, 'fsdp', axis=0, tiled=True)  55.9 us
    all_gather x1, waiting for transfers between devices, per_device(): lax.all_gather(w_key, 'fsdp', axis=0, tiled=True)  41.2 us
    all_to_all x1, waiting for transfers between devices, per_device(): lax.all_to_all(found, ('grp', 'fsdp'), split_axis=0, concat_axis=0, tiled...  17.7 us
    all_to_all x1, waiting for transfers between devices, per_device(): lax.all_to_all(outgoing.reshape(devices, cap_slots, DI).astype(jnp.bfloat...  16.4 us
    dot_general x1, matrix products, per_device(): jnp.dot(grad_hidden, adapter.T, preferred_element_type=jnp.float32)  12.5 us
  transfers between devices with their start and end apart: 8, of which 8 were waited for; matrix products, arithmetic and copies ran while one was open for 7% of the time, Pallas kernels for 0%

commit v1 on v0

--- a/solution.py
+++ b/solution.py
@@ -91,7 +91,9 @@
     columns = last_row
     query_sum = jnp.dot(
         columns,
-        lax.all_gather(w_query, "fsdp", axis=0, tiled=True),
+        jnp.concatenate(
+            lax.all_to_all(jnp.stack([w_query] * lax.axis_size("fsdp")), "fsdp", 0, 0), axis=0
+        ),
         preferred_element_type=jnp.float32,
     )
     adapter, query_map = (

time: 474 us -> 492 us (1.038)
  blocking collectives: 0 us -> 20.7 us
  starting transfers between devices: 27.4 us -> 21.2 us
    all_gather x1, waiting for transfers between devices: 41.2 us -> 124 us  [per_device(): lax.all_gather(w_key, 'fsdp', axis=0, tiled=True)]
    all_gather x1 -> x0, waiting for transfers between devices: 76.3 us -> none  [per_device(): lax.all_gather(w_query, 'fsdp', axis=0, tiled=True)]
    all_to_all x0 -> x1, blocking collectives: none -> 20.7 us  [per_device(): lax.all_to_all(request, ('grp', 'fsdp'), split_axis=0, concat_axis=0, til...]
    all_to_all x1, waiting for transfers between devices: 8.22 us -> 0.01 us  [per_device(): lax.all_to_all(jnp.stack([w_query] * lax.axis_size('fsdp')), 'fsdp', 0, 0)]
    all_to_all x1, starting transfers between devices: 11.5 us -> 5.75 us  [per_device(): lax.all_to_all(jnp.stack([w_query] * lax.axis_size('fsdp')), 'fsdp', 0, 0)]
    another operation x0 -> x1, local copies, waits for them, and re-layouts: none -> 5.17 us  [per_device(): jnp.stack([w_query] * lax.axis_size('fsdp'))]
  transfers between devices with their start and end apart: 8 -> 7, of which waited for: 8 -> 6; matrix products, arithmetic and copies ran while one was open for 7% -> 8% of each run, Pallas kernels for 0% -> 0%
where the time goes in v1:
time: 492 us; the launch traced here: 491 us
  waiting for transfers between devices  356 us (72%)
  matrix products  47.8 us (10%)
  local copies, waits for them, and re-layouts  21.5 us (4%)
  starting transfers between devices  21.2 us (4%)
  blocking collectives  20.7 us (4%)
  between operations  14.1 us (3%)
  other arithmetic  9.93 us (2%)
    all_gather x1, waiting for transfers between devices, per_device(): lax.all_gather(w_key, 'fsdp', axis=0, tiled=True)  124 us
    all_gather x1, waiting for transfers between devices, per_device(): lax.all_gather(w_adapt, 'fsdp', axis=0, tiled=True)  76.6 us
    all_gather x1, waiting for transfers between devices, per_device(): lax.all_gather(w_value, 'fsdp', axis=0, tiled=True)  63.9 us
    all_gather x1, waiting for transfers between devices, per_device(): lax.all_gather(user_query, 'fsdp', axis=0, tiled=True)  55.9 us
    all_to_all x1, blocking collectives, per_device(): lax.all_to_all(request, ('grp', 'fsdp'), split_axis=0, concat_axis=0, til...  20.7 us
    all_to_all x1, waiting for transfers between devices, per_device(): lax.all_to_all(found, ('grp', 'fsdp'), split_axis=0, concat_axis=0, tiled...  16.8 us
    all_to_all x1, waiting for transfers between devices, per_device(): lax.all_to_all(outgoing.reshape(devices, cap_slots, DI).astype(jnp.bfloat...  16.4 us
    dot_general x1, matrix products, per_device(): jnp.dot(grad_hidden, adapter.T, preferred_element_type=jnp.float32)  12.5 us
  transfers between devices with their start and end apart: 7, of which 6 were waited for; matrix products, arithmetic and copies ran while one was open for 8% of the time, Pallas kernels for 0%

profile of v1, /device:TPU:1, one launch (start us, length us, event | category | flops | bytes accessed | tf_op | source)
XLA Modules:
  0.0 490.9 jit_solution(1776051180005693340)
XLA Ops:
  7.2 0.7 all-gather.5.cloned.1.call-update
  7.9 0.7 all-gather.7.cloned.1.call-update
  8.7 0.7 all-gather.9.cloned.1.call-update
  9.4 0.7 fusion.54
  10.1 0.2 reduce_window_sum.11
  10.3 0.8 select_reduce_fusion
  11.1 0.7 fusion.58
  11.8 1.1 scatter_custom_fusion
  12.9 0.1 all_to_all.16
  13.1 20.7 %all_to_all.24 = s32[128,1,2]{2,1,0:T(1,128)S(1)} all-to-all(s32[128,1,2]{2,1,0:T(1,128)S(1)} %bitcast.113), channel_id=1, replica_groups=mesh['grp'=2,'fsdp'=64] {'grp','fsdp'}, dimensions={0} | all-to-all | bytes 2048 | tf_op jit(solution)/shard_map/all_to_all | solution.py:122
  33.7 5.2 %stack.2 = bf16[64,32,2048]{2,1,0:T(8,128)(2,1)} broadcast(bf16[32,2048]{1,0:T(8,128)(2,1)} %param.12), dimensions={1,2} | broadcast | bytes 8519680 | tf_op jit(solution)/shard_map/stack | solution.py:95
  38.9 5.7 %all-to-all-start = ((bf16[64,32,2048]{2,1,0:T(8,128)(2,1)}), bf16[64,32,2048]{2,1,0:T(8,128)(2,1)}, u32[]{:S(2)}, u32[]{:S(2)}) async-start(bf16[64,32,2048]{2,1,0:T(8,128)(2,1)} %stack.2), calls=%async_computation | async-start | bytes 16777216 | tf_op jit(solution)/shard_map/all_to_all | solution.py:95
  44.6 0.9 slice.4
  45.6 0.1 reshape.163
  45.8 123.5 %all-gather.5.cloned.1.call-done = bf16[2048,256]{1,0:T(8,128)(2,1)} async-done(((bf16[32,256]{1,0:T(8,128)(2,1)}), bf16[2048,256]{1,0:T(8,128)(2,1)}) %all-gather.5.cloned.1.call-update) | async-done | bytes 1048592 | tf_op jit(solution)/shard_map/all_gather | solution.py:83
  169.3 3.7 convolution_convert_fusion.7
  173.1 0.4 reshape.189
  173.5 63.9 %all-gather.7.cloned.1.call-done = bf16[2048,256]{1,0:T(8,128)(2,1)} async-done(((bf16[32,256]{1,0:T(8,128)(2,1)}), bf16[2048,256]{1,0:T(8,128)(2,1)}) %all-gather.7.cloned.1.call-update) | async-done | bytes 1048592 | tf_op jit(solution)/shard_map/all_gather | solution.py:88
  237.4 3.7 convolution_convert_fusion.6
  241.1 0.4 reshape.190
  241.6 4.6 convolution_convert_fusion.2
  246.1 0.1 reshape.152
  246.2 0.6 fusion.75
  246.8 0.1 divide_convert_fusion.1
  246.9 0.3 multiply_reduce_fusion
  247.4 0.5 convolution_convert_fusion.1
  248.0 2.0 copy.53
  250.0 7.6 %all-to-all-start.2 = ((bf16[128,2,2048]{2,1,0:T(2,128)(2,1)}), bf16[128,2,2048]{2,1,0:T(2,128)(2,1)S(1)}, u32[]{:S(2)}, u32[]{:S(2)}) async-start(bf16[128,2,2048]{2,1,0:T(2,128)(2,1)} %copy.53), calls=%async_computation.2 | async-start | bytes 2097152 | tf_op jit(solution)/shard_map/all_to_all | solution.py:124
  257.6 0.2 all-gather.11.cloned.1.call-start
  257.8 0.3 all-gather.11.cloned.1.call-update
  258.2 0.7 copy.79
  258.9 16.8 %all-to-all-done.2 = bf16[128,2,2048]{2,1,0:T(2,128)(2,1)S(1)} async-done(((bf16[128,2,2048]{2,1,0:T(2,128)(2,1)}), bf16[128,2,2048]{2,1,0:T(2,128)(2,1)S(1)}, u32[]{:S(2)}, u32[]{:S(2)}) %all-to-all-start.2) | async-done | bytes 1048608 | tf_op jit(solution)/shard_map/all_to_all | solution.py:124
  275.8 0.4 reshape.157
  276.2 0.9 gather_fusion
  277.1 76.6 %all-gather.9.cloned.1.call-done = bf16[2048,4096]{1,0:T(8,128)(2,1)} async-done(((bf16[32,4096]{1,0:T(8,128)(2,1)}), bf16[2048,4096]{1,0:T(8,128)(2,1)}) %all-gather.9.cloned.1.call-update) | async-done | bytes 16777232 | tf_op jit(solution)/shard_map/all_gather | solution.py:100
  353.8 8.2 %convolution_convert_fusion = bf16[128,4096]{1,0:T(8,128)(2,1)S(1)} fusion(bf16[2048,4096]{1,0:T(8,128)(2,1)} %all-gather.9.cloned.1.call-done, bf16[128,2048]{1,0:T(8,128)(2,1)S(1)} %gather_fusion, pred[128]{0:T(512)(128)(4,1)S(1)} %compare_and_fusion), kind=kOutput, calls=%fused_computation.5 | convolution fusion | flops 2148270080 | bytes 18350208 | tf_op jit(solution)/shard_map/dot_general | solution.py:126
  361.9 0.3 fusion.9
  362.2 0.3 fusion.11
  362.6 55.9 %all-gather.11.cloned.1.call-done = bf16[4096,128]{1,0:T(8,128)(2,1)} async-done(((bf16[64,128]{1,0:T(8,128)(2,1)}), bf16[4096,128]{1,0:T(8,128)(2,1)}) %all-gather.11.cloned.1.call-update) | async-done | bytes 1048592 | tf_op jit(solution)/shard_map/all_gather | solution.py:101
  418.5 2.6 fusion.15
  421.1 1.4 fusion.16
  422.5 3.5 fusion.76
  426.0 2.6 fusion.7
  428.7 0.2 copy-done.4
  428.9 0.3 copy-done.5
  429.1 0.8 fusion.73
  430.0 0.8 fusion.17
  430.8 0.9 fusion.81
  431.6 1.9 fusion.29
  433.5 0.9 add_convert_fusion
  434.4 0.5 copy.80
  434.9 2.9 copy.78
  437.8 3.1 fusion.13
  441.0 12.5 %fusion.22 = f32[128,2048]{1,0:T(8,128)} fusion(bf16[2048,4096]{1,0:T(8,128)(2,1)} %all-gather.9.cloned.1.call-done, bf16[128,4096]{1,0:T(8,128)(2,1)S(1)} %convolution_convert_fusion, bf16[128,4096]{1,0:T(8,128)(2,1)S(1)} %copy.80, bf16[1,128,4096]{2,1,0:T(8,128)(2,1)S(1)} %copy-done.2, f32[128]{0:T(128)S(1)} %multiply_multiply_fusion, ...), kind=kOutput, calls=%fused_computation.47 | convolution fusion | flops 2152202240 | bytes 20988928 | tf_op jit(solution)/shard_map/dot_general | solution.py:131
  453.4 2.4 scatter_custom_fusion.1
  455.8 0.1 convert_element_type.129
  456.0 1.5 convert_element_type.130
  457.5 7.6 %all-to-all-start.3 = ((bf16[128,2,2048]{2,1,0:T(2,128)(2,1)}), bf16[128,2,2048]{2,1,0:T(2,128)(2,1)S(1)}, u32[]{:S(2)}, u32[]{:S(2)}) async-start(bf16[128,2,2048]{2,1,0:T(2,128)(2,1)} %convert_element_type.130), calls=%async_computation.3 | async-start | bytes 2097152 | tf_op jit(solution)/shard_map/all_to_all | solution.py:133
  465.1 0.5 broadcast.138
  465.6 0.8 reduce.4
  466.4 0.1 eq.50
  466.6 16.4 %all-to-all-done.3 = bf16[128,2,2048]{2,1,0:T(2,128)(2,1)S(1)} async-done(((bf16[128,2,2048]{2,1,0:T(2,128)(2,1)}), bf16[128,2,2048]{2,1,0:T(2,128)(2,1)S(1)}, u32[]{:S(2)}, u32[]{:S(2)}) %all-to-all-start.3) | async-done | bytes 1048608 | tf_op jit(solution)/shard_map/all_to_all | solution.py:133
  482.9 0.4 reshape.162
  483.4 1.0 fusion.52
  (34 shorter events, 0.5 us)
Async XLA Ops:
  7.2 162.2 %all-gather.5.cloned.1.call-start = ((), (), s32[]{:S(2)}) async-start(), calls=%async_computation.4 | async-start | bytes 1064960 | tf_op jit(solution)/shard_map/all_gather | solution.py:83
  7.9 229.5 %all-gather.7.cloned.1.call-start = ((), (), s32[]{:S(2)}) async-start(), calls=%async_computation.5 | async-start | bytes 1064960 | tf_op jit(solution)/shard_map/all_gather | solution.py:88
  8.6 345.1 %all-gather.9.cloned.1.call-start = ((), (), s32[]{:S(2)}) async-start(), calls=%async_computation.6 | async-start | bytes 17039360 | tf_op jit(solution)/shard_map/all_gather | solution.py:100
  38.9 202.7 %all-to-all-start = ((bf16[64,32,2048]{2,1,0:T(8,128)(2,1)}), bf16[64,32,2048]{2,1,0:T(8,128)(2,1)}, u32[]{:S(2)}, u32[]{:S(2)}) async-start(bf16[64,32,2048]{2,1,0:T(8,128)(2,1)} %stack.2), calls=%async_computation | async-start | bytes 16777216 | tf_op jit(solution)/shard_map/all_to_all | solution.py:95
  246.1 1.2 copy-start.8
  247.4 2.6 copy-start.7
  248.0 10.2 %copy-start.1 = (bf16[1,128,4096]{2,1,0:T(8,128)(2,1)S(1)}, bf16[1,128,4096]{2,1,0:T(8,128)(2,1)}, u32[]{:S(2)}) copy-start(bf16[1,128,4096]{2,1,0:T(8,128)(2,1)} %param.21) | copy-start | bytes 3145732
  250.0 8.9 %copy-start.9 = (s32[1,128,1]{1,2,0:T(1,128)S(1)}, s32[1,128,1]{1,2,0:T(1,128)}, u32[]{:S(2)}) copy-start(s32[1,128,1]{1,2,0:T(1,128)} %param.19) | copy-start | bytes 1540
  250.0 25.7 %all-to-all-start.2 = ((bf16[128,2,2048]{2,1,0:T(2,128)(2,1)}), bf16[128,2,2048]{2,1,0:T(2,128)(2,1)S(1)}, u32[]{:S(2)}, u32[]{:S(2)}) async-start(bf16[128,2,2048]{2,1,0:T(2,128)(2,1)} %copy.53), calls=%async_computation.2 | async-start | bytes 2097152 | tf_op jit(solution)/shard_map/all_to_all | solution.py:124
  257.6 160.8 %all-gather.11.cloned.1.call-start = ((), (), s32[]{:S(2)}) async-start(), calls=%async_computation.7 | async-start | bytes 1064960 | tf_op jit(solution)/shard_map/all_gather | solution.py:101
  277.1 85.1 %copy-start.6 = (f32[4096]{0:T(1024)S(1)}, f32[4096]{0:T(1024)}, u32[]{:S(2)}) copy-start(f32[4096]{0:T(1024)} %param.17) | copy-start | bytes 49156
  426.0 2.6 copy-start.3
  426.0 2.9 copy-start.4
  426.0 3.1 copy-start.5
  431.6 1.9 copy-start
  437.8 3.1 copy-start.2
  457.5 25.4 %all-to-all-start.3 = ((bf16[128,2,2048]{2,1,0:T(2,128)(2,1)}), bf16[128,2,2048]{2,1,0:T(2,128)(2,1)S(1)}, u32[]{:S(2)}, u32[]{:S(2)}) async-start(bf16[128,2,2048]{2,1,0:T(2,128)(2,1)} %convert_element_type.130), calls=%async_computation.3 | async-start | bytes 2097152 | tf_op jit(solution)/shard_map/all_to_all | solution.py:133
Sparse Core Ops, SparseCore 0:
  10.9 158.4 all-gather.4
  172.2 65.1 all-gather.6
  240.3 113.4 all-gather.8
  356.5 61.9 all-gather.10
